TPU v7x, 128 devices: a whole 4x4x4 slice. The times are simulated.
128 devices in a mesh: dp: 16 (over y, z_lo, core), tensor: 8 (over z_hi, x).
Axes of the slice: x: 4, y: 4, z: 4 (z_hi: 2, z_lo: 2; z = z_hi * 2 + z_lo), core: 2. Of those that a mesh axis runs over, the one named last changes fastest.
Arguments:
- stream: bfloat16 [16384, 2048], P(('dp', 'tensor')), may hold values from -6 to 6
- segment: int32 [16384], P('dp'), may hold values from -1 to 16383, as said below
- position: int32 [16384], P('dp'), may hold values from 0 to 4606, as said below
- w_qkv: bfloat16 [3, 2048, 2048], P(None, 'dp', 'tensor'), may hold values from -0.5 to 0.5
- w_out: bfloat16 [2048, 2048], P('tensor', 'dp'), may hold values from -0.125 to 0.125
- w_gate_up: bfloat16 [2, 2048, 8192], P(None, 'dp', 'tensor'), may hold values from -0.125 to 0.125
- w_down: bfloat16 [8192, 2048], P('tensor', 'dp'), may hold values from -0.0625 to 0.0625
- page_table: int32 [1024], P('dp'), may hold values from 0 to 1023, as said below
Outputs:
- layer_out: bfloat16 [16384, 2048], P(('dp', 'tensor'))
- kv_cache: bfloat16 [1024, 2, 16, 2048], P('dp', None, None, 'tensor')
Inputs may be any that keep to these rules, and one draw needn't show every extreme that they name: `segment`: each group's tokens form prompts of 64 to 512 tokens with distinct numbers, laid one after another, followed by padding -1 at the end of the group's stream; some prompt has 512 tokens in every group. Within a prompt positions rise by one from a first position below 4096; padding has position 0; in every group some prompt of 512 tokens starts at 4095. `page_table`: A permutation of all 1024 page ids. Among the 64 blocks of one request group, exactly 4 fall into each of the ranges o * 64 to (o + 1) * 64 - 1.
All inputs are finite; a program needn't handle non-finite values.
Results may differ from a plain program's by a relative error of at most 0.015.
Values may be sent and summed in bfloat16 or wider, within the bound.
No kernel may reach another device: no remote copies, remote signals or barrier semaphores. Data moves between devices by JAX's collectives and lax.ppermute only.
A program may use at most 128 MiB of HBM per device.

v0:
```python
import math
import jax
import jax.numpy as jnp
from jax import lax
from jax.sharding import PartitionSpec as P

HD = 128


def layer_norm(values):
    values = values.astype(jnp.float32)
    center = values - jnp.mean(values, axis=-1, keepdims=True)
    spread = jnp.mean(center * center, axis=-1, keepdims=True)
    return center * lax.rsqrt(spread + 1e-05)


def rotate(values, position):
    half = values.shape[-1] // 2
    freq = 10000.0 ** (-jnp.arange(half, dtype=jnp.float32) * 2.0 / values.shape[-1])
    angle = position.astype(jnp.float32)[:, None] * freq[None, :]
    cosine = jnp.cos(angle)[:, None, :]
    sine = jnp.sin(angle)[:, None, :]
    first = values[..., :half]
    second = values[..., half:]
    return jnp.concatenate(
        [first * cosine - second * sine, second * cosine + first * sine], axis=-1
    )


def row_folder(source, piece):
    return jnp.einsum("td,cdf->ctf", source, piece, preferred_element_type=jnp.float32)


def attend(query, keys, values, segment):
    tokens = query.shape[0]
    block = min(512, tokens)
    scale = 1.0 / math.sqrt(HD)
    order = jnp.arange(tokens)
    outputs = []
    for first in range(0, tokens, block):
        last = first + block
        scores = (
            jnp.einsum(
                "qhd,khd->hqk", query[first:last], keys[:last], preferred_element_type=jnp.float32
            )
            * scale
        )
        allowed = (segment[first:last, None] == segment[None, :last]) & (
            order[None, :last] <= order[first:last, None]
        )
        top = jnp.max(jnp.where(allowed[None], scores, -1e30), axis=-1, keepdims=True)
        weights = jnp.exp(jnp.where(allowed[None], scores - top, -1e30))
        total = jnp.sum(weights, axis=-1)
        mixed = jnp.einsum(
            "hqk,khd->qhd",
            weights.astype(jnp.bfloat16),
            values[:last],
            preferred_element_type=jnp.float32,
        )
        outputs.append((mixed / jnp.transpose(total)[:, :, None]).astype(jnp.bfloat16))
    return jnp.concatenate(outputs, axis=0).reshape(tokens, -1)


def write_cache(keys, values, page_table):
    tokens = keys.shape[0]
    width = keys.shape[1] * keys.shape[2]
    pages = page_table.shape[0]
    page_size = tokens // pages
    owners = lax.axis_size("dp")
    per_owner = pages // owners
    stacked = jnp.stack([keys.reshape(tokens, width), values.reshape(tokens, width)], axis=0)
    stacked = stacked.reshape(2, pages, page_size, width).transpose(1, 0, 2, 3)
    order = jnp.argsort(page_table // pages, stable=True)
    outgoing = stacked[order].reshape(owners, per_owner, 2, page_size, width)
    outgoing_ids = page_table[order].reshape(owners, per_owner)
    arrived, arrived_ids = (
        lax.all_to_all(outgoing, "dp", split_axis=0, concat_axis=0, tiled=True),
        lax.all_to_all(outgoing_ids, "dp", split_axis=0, concat_axis=0, tiled=True),
    )
    local = (arrived_ids - lax.axis_index("dp") * pages).reshape(-1)
    empty = jnp.zeros((pages, 2, page_size, width), jnp.bfloat16)
    return empty.at[local].set(arrived.reshape(pages, 2, page_size, width))


def body(stream, segment, position, w_qkv, w_out, w_gate_up, w_down, page_table):
    tok_group = segment.shape[0]
    share_rows = stream.shape[0]
    full_stream = lax.all_gather(stream, "tensor", axis=0, tiled=True)
    normed = layer_norm(full_stream).astype(jnp.bfloat16)
    local_heads = w_qkv.shape[2] // HD
    projected = row_folder(normed, lax.all_gather(w_qkv, "dp", axis=1, tiled=True))
    query = rotate(projected[0].reshape(tok_group, local_heads, HD), position).astype(jnp.bfloat16)
    keys = rotate(projected[1].reshape(tok_group, local_heads, HD), position).astype(jnp.bfloat16)
    values = projected[2].reshape(tok_group, local_heads, HD).astype(jnp.bfloat16)
    context = attend(query, keys, values, segment)
    attn_part = jnp.dot(
        context, lax.all_gather(w_out, "dp", axis=1, tiled=True), preferred_element_type=jnp.float32
    )
    attn_whole = lax.psum(attn_part.astype(jnp.bfloat16), "tensor").astype(jnp.float32)
    mid = (full_stream.astype(jnp.float32) + attn_whole).astype(jnp.bfloat16)
    normed2 = layer_norm(mid).astype(jnp.bfloat16)
    gate_up = row_folder(normed2, lax.all_gather(w_gate_up, "dp", axis=1, tiled=True))
    hidden = (jax.nn.silu(gate_up[0]) * gate_up[1]).astype(jnp.bfloat16)
    mlp_part = jnp.dot(
        hidden, lax.all_gather(w_down, "dp", axis=1, tiled=True), preferred_element_type=jnp.float32
    )
    mlp_whole = lax.psum(mlp_part.astype(jnp.bfloat16), "tensor").astype(jnp.float32)
    result = (mid.astype(jnp.float32) + mlp_whole).astype(jnp.bfloat16)
    layer_out = lax.dynamic_slice_in_dim(
        result, lax.axis_index("tensor") * share_rows, share_rows, 0
    )
    kv_cache = write_cache(keys, values, page_table)
    return (layer_out, kv_cache)


def solution(mesh):
    return jax.shard_map(
        body,
        mesh=mesh,
        in_specs=(
            P(("dp", "tensor"), None),
            P("dp"),
            P("dp"),
            P(None, "dp", "tensor"),
            P("tensor", "dp"),
            P(None, "dp", "tensor"),
            P("tensor", "dp"),
            P("dp"),
        ),
        out_specs=(P(("dp", "tensor"), None), P("dp", None, None, "tensor")),
        check_vma=False,
    )
```

profile of v0, /device:TPU:1, one launch (start us, length us, event | category | flops | bytes accessed | tf_op | source)
XLA Modules:
  0.0 515.2 jit_solution(17798327678414374484)
XLA Ops:
  7.2 0.7 all-gather.6.cloned.1.call-update
  7.9 1.7 copy.27
  9.8 0.7 all-gather.10.cloned.1.call-update
  10.5 0.7 convert_element_type.76
  11.2 0.8 fusion.83
  12.0 1.9 multiply_cosine_fusion
  14.2 2.1 fusion.35
  16.2 68.2 %all-gather.6.cloned.1.call-done = bf16[1024,2048]{1,0:T(8,128)(2,1)} async-done(((bf16[128,2048]{1,0:T(8,128)(2,1)}), bf16[1024,2048]{1,0:T(8,128)(2,1)}) %all-gather.6.cloned.1.call-update) | async-done | bytes 4194320 | tf_op jit(solution)/shard_map/all_gather | solution.py:88
  84.4 3.0 convert_reduce_fusion
  87.9 1.2 fusion.4
  89.1 37.2 %all-gather.8.cloned.1.call-done = bf16[3,2048,256]{1,2,0:T(8,128)(2,1)} async-done(((bf16[3,128,256]{1,2,0:T(8,128)(2,1)}), bf16[3,2048,256]{1,2,0:T(8,128)(2,1)}) %all-gather.8.cloned.1.call-update) | async-done | bytes 3145744 | tf_op jit(solution)/shard_map/all_gather | solution.py:91
  126.3 7.3 %fusion.38 = f32[3,1024,256]{1,2,0:T(8,128)S(1)} fusion(bf16[3,2048,256]{1,2,0:T(8,128)(2,1)} %all-gather.8.cloned.1.call-done, bf16[1024,2048]{1,0:T(8,128)(2,1)} %all-gather.6.cloned.1.call-done, f32[1024]{0:T(1024)S(1)} %add_rsqrt_fusion.1, f32[1024]{0:T(1024)S(1)} %broadcast_multiply_fusion.1), kind=kOutput, calls=%fused_computation.47 | convolution fusion | flops 3229614080 | bytes 10493952 | tf_op jit(solution)/shard_map/td,cdf->ctf/dot_general | solution.py:31
  133.9 0.9 slice.112
  134.8 1.0 fusion.81
  135.8 1.4 copy.41
  137.2 2.4 copy.42
  139.5 1.1 fusion.82
  140.6 1.4 copy.39
  142.0 2.4 copy.40
  144.4 1.6 multiply_subtract_fusion
  146.6 0.8 copy-done.7
  147.9 1.3 copy-done.6
  149.2 1.1 fusion.85
  150.3 3.4 fusion.48
  153.7 3.9 fusion.84
  157.6 2.5 fusion.49
  160.1 1.8 all-gather.10.cloned.1.call-done
  161.9 4.5 convolution_convert_fusion
  167.9 108.5 %all-reduce.3.cloned.1.call-done = bf16[1024,2048]{1,0:T(8,128)(2,1)} async-done(((bf16[1024,2048]{1,0:T(8,128)(2,1)}), bf16[1024,2048]{1,0:T(8,128)(2,1)}) %all-reduce.3.cloned.1.call-update) | async-done | bytes 4194320 | tf_op jit(solution)/shard_map/psum | solution.py:99
  276.4 4.8 convert_reduce_fusion.1
  281.1 1.9 copy-done.1
  283.1 1.2 multiply_reduce_fusion
  284.3 44.9 %all-gather.12.cloned.1.call-done = bf16[2,2048,1024]{2,1,0:T(8,128)(2,1)} async-done(((bf16[2,128,1024]{2,1,0:T(8,128)(2,1)}), bf16[2,2048,1024]{2,1,0:T(8,128)(2,1)}) %all-gather.12.cloned.1.call-update) | async-done | bytes 8388624 | tf_op jit(solution)/shard_map/all_gather | solution.py:102
  329.2 14.6 %fusion.23 = f32[2,1024,1024]{2,1,0:T(8,128)} fusion(bf16[2,2048,1024]{2,1,0:T(8,128)(2,1)} %all-gather.12.cloned.1.call-done, bf16[1024,2048]{1,0:T(8,128)(2,1)} %copy-done.1, f32[1024]{0:T(1024)S(1)} %add_rsqrt_fusion, f32[1024]{0:T(1024)S(1)} %broadcast_multiply_fusion), kind=kOutput, calls=%fused_computation.34 | convolution fusion | flops 8598323200 | bytes 20979712 | tf_op jit(solution)/shard_map/td,cdf->ctf/dot_general | solution.py:31
  343.8 32.8 %all-gather.14.cloned.1.call-done = bf16[1024,2048]{1,0:T(8,128)(2,1)} async-done(((bf16[1024,128]{1,0:T(8,128)(2,1)}), bf16[1024,2048]{1,0:T(8,128)(2,1)}) %all-gather.14.cloned.1.call-update) | async-done | bytes 4194320 | tf_op jit(solution)/shard_map/all_gather | solution.py:105
  376.5 11.2 %convolution_convert_fusion.1 = bf16[1024,2048]{1,0:T(8,128)(2,1)} fusion(bf16[1024,2048]{1,0:T(8,128)(2,1)} %all-gather.14.cloned.1.call-done, f32[2,1024,1024]{2,1,0:T(8,128)} %fusion.23), kind=kOutput, calls=%fused_computation.32 | convolution fusion | flops 4303355904 | bytes 16777216 | tf_op jit(solution)/shard_map/dot_general | solution.py:104
  388.4 2.0 sort.17
  390.4 0.8 gather_fusion
  391.2 0.7 all_to_all.9
  391.9 4.3 all-to-all-start
  397.4 1.6 gather_fusion.1
  398.9 2.7 all-to-all-done
  401.7 4.1 all-to-all-start.1
  405.9 45.7 %all-to-all-done.1 = bf16[16,4,2,16,256]{4,3,2,1,0:T(8,128)(2,1)S(1)} async-done(((bf16[16,4,2,16,256]{4,3,2,1,0:T(8,128)(2,1)}), bf16[16,4,2,16,256]{4,3,2,1,0:T(8,128)(2,1)S(1)}, u32[]{:S(2)}, u32[]{:S(2)}) %all-to-all-start.1) | async-done | bytes 1048608 | tf_op jit(solution)/shard_map/all_to_all | solution.py:77
  451.7 2.5 scatter_fusion
  454.2 6.8 %convert_element_type.86 = f32[1024,2048]{1,0:T(8,128)} convert(bf16[1024,2048]{1,0:T(8,128)(2,1)} %copy-done.1) | non-fusion elementwise | flops 2097152 | bytes 12582912 | tf_op jit(solution)/shard_map/convert_element_type | solution.py:108
  461.1 45.0 %all-reduce.5.cloned.1.call-done = bf16[1024,2048]{1,0:T(8,128)(2,1)} async-done(((bf16[1024,2048]{1,0:T(8,128)(2,1)}), bf16[1024,2048]{1,0:T(8,128)(2,1)}) %all-reduce.5.cloned.1.call-update) | async-done | bytes 4194320 | tf_op jit(solution)/shard_map/psum | solution.py:107
  506.1 2.3 fusion.52
  (58 shorter events, 5.9 us)
Async XLA Ops:
  7.2 77.3 %all-gather.6.cloned.1.call-start = ((), (), s32[]{:S(2)}) async-start(), calls=%async_computation.2 | async-start | bytes 4718592 | tf_op jit(solution)/shard_map/all_gather | solution.py:88
  7.9 118.4 %all-gather.8.cloned.1.call-start = ((), (), s32[]{:S(2)}) async-start(), calls=%async_computation.3 | async-start | bytes 3342336 | tf_op jit(solution)/shard_map/all_gather | solution.py:91
  9.7 152.2 %all-gather.10.cloned.1.call-start = ((), (), s32[]{:S(2)}) async-start(), calls=%async_computation.4 | async-start | bytes 1114112 | tf_op jit(solution)/shard_map/all_gather | solution.py:97
  10.4 265.9 %all-reduce.3.cloned.1.call-start = ((), (), s32[]{:S(2)}) async-start(), calls=%async_computation.5 | async-start | bytes 8388608 | tf_op jit(solution)/shard_map/psum | solution.py:99
  84.4 3.4 copy-start.2
  144.4 1.9 copy-start.4
  146.5 0.8 copy-start.7
  147.3 2.9 slice-start
  147.9 1.3 copy-start.6
  149.2 4.5 copy-start.8
  149.2 4.5 copy-start.9
  153.7 3.9 copy-start.5
  166.4 162.8 %all-gather.12.cloned.1.call-start = ((), (), s32[]{:S(2)}) async-start(), calls=%async_computation.6 | async-start | bytes 8912896 | tf_op jit(solution)/shard_map/all_gather | solution.py:102
  167.0 209.5 %all-gather.14.cloned.1.call-start = ((), (), s32[]{:S(2)}) async-start(), calls=%async_computation.7 | async-start | bytes 4456448 | tf_op jit(solution)/shard_map/all_gather | solution.py:105
  167.6 338.5 %all-reduce.5.cloned.1.call-start = ((), (), s32[]{:S(2)}) async-start(), calls=%async_computation.8 | async-start | bytes 8388608 | tf_op jit(solution)/shard_map/psum | solution.py:107
  281.1 1.9 copy-start.1
  387.7 0.7 copy-start
  391.9 9.8 %all-to-all-start = ((s32[16,1,4]{2,1,0:T(1,128)}), s32[16,1,4]{2,1,0:T(1,128)S(1)}, u32[]{:S(2)}, u32[]{:S(2)}) async-start(s32[16,1,4]{2,1,0:T(1,128)} %bitcast.15), calls=%async_computation | async-start | bytes 16384 | tf_op jit(solution)/shard_map/all_to_all | solution.py:78
  401.7 49.9 %all-to-all-start.1 = ((bf16[16,4,2,16,256]{4,3,2,1,0:T(8,128)(2,1)}), bf16[16,4,2,16,256]{4,3,2,1,0:T(8,128)(2,1)S(1)}, u32[]{:S(2)}, u32[]{:S(2)}) async-start(bf16[16,4,2,16,256]{4,3,2,1,0:T(8,128)(2,1)} %bitcast.21), calls=%async_computation.1 | async-start | bytes 2097152 | tf_op jit(solution)/shard_map/all_to_all | solution.py:77
  454.2 6.9 %copy-start.3 = (bf16[64,2,16,256]{3,2,1,0:T(8,128)(2,1)}, bf16[64,2,16,256]{3,2,1,0:T(8,128)(2,1)S(1)}, u32[]{:S(2)}) copy-start(bf16[64,2,16,256]{3,2,1,0:T(8,128)(2,1)S(1)} %scatter_fusion) | copy-start | bytes 3145732
Sparse Core Ops, SparseCore 0:
  10.3 74.0 all-gather.5
  86.6 39.6 all-gather.7
  127.9 33.9 all-gather.9
  166.6 109.7 all-reduce.2
  277.9 51.2 all-gather.11
  330.7 45.8 all-gather.13
  387.9 118.1 all-reduce.4
where the time goes:
time: 516 us; the launch traced here: 515 us
  waiting for transfers between devices  389 us (75%)
  matrix products  47.9 us (9%)
  other arithmetic  29.7 us (6%)
  local copies, waits for them, and re-layouts  25.2 us (5%)
  between operations  14.4 us (3%)
  starting transfers between devices  8.88 us (2%)
    psum x1, waiting for transfers between devices, body(): lax.psum(attn_part.astype(jnp.bfloat16), 'tensor').astype(jnp.float32)  108 us
    all_gather x1, waiting for transfers between devices, body(): full_stream = lax.all_gather(stream, 'tensor', axis=0, tiled=True)  68.2 us
    all_to_all x1, waiting for transfers between devices, write_cache(): lax.all_to_all(outgoing, 'dp', split_axis=0, concat_axis=0, tiled=True)  45.7 us
    psum x1, waiting for transfers between devices, body(): lax.psum(mlp_part.astype(jnp.bfloat16), 'tensor').astype(jnp.float32)  45 us
    all_gather x1, waiting for transfers between devices, body(): lax.all_gather(w_gate_up, 'dp', axis=1, tiled=True)  44.9 us
    all_gather x1, waiting for transfers between devices, body(): lax.all_gather(w_qkv, 'dp', axis=1, tiled=True)  37.2 us
    all_gather x1, waiting for transfers between devices, body(): lax.all_gather(w_down, 'dp', axis=1, tiled=True)  32.8 us
    dot_general x2, matrix products, row_folder(): jnp.einsum('td,cdf->ctf', source, piece, preferred_element_type=jnp.float32)  21.9 us
  transfers between devices with their start and end apart: 9, of which 9 were waited for; matrix products, arithmetic and copies ran while one was open for 15% of the time, Pallas kernels for 0%

commit v1 on v0

--- a/solution.py
+++ b/solution.py
@@ -104,7 +104,9 @@
     mlp_part = jnp.dot(
         hidden, lax.all_gather(w_down, "dp", axis=1, tiled=True), preferred_element_type=jnp.float32
     )
-    mlp_whole = lax.psum(mlp_part.astype(jnp.bfloat16), "tensor").astype(jnp.float32)
+    mlp_whole = jnp.sum(lax.all_gather(mlp_part.astype(jnp.bfloat16), "tensor"), axis=0).astype(
+        jnp.float32
+    )
     result = (mid.astype(jnp.float32) + mlp_whole).astype(jnp.bfloat16)
     layer_out = lax.dynamic_slice_in_dim(
         result, lax.axis_index("tensor") * share_rows, share_rows, 0

time: 516 us -> 762 us (1.48)
  waiting for transfers between devices: 389 us -> 621 us
  other arithmetic: 29.7 us -> 43.8 us
    all_gather x0 -> x1, waiting for transfers between devices: none -> 305 us  [body(): lax.all_gather(mlp_part.astype(jnp.bfloat16), 'tensor')]
    psum x1 -> x0, waiting for transfers between devices: 45 us -> none  [body(): lax.psum(mlp_part.astype(jnp.bfloat16), 'tensor').astype(jnp.float32)]
    all_to_all x1, waiting for transfers between devices: 45.7 us -> 17.3 us  [write_cache(): lax.all_to_all(outgoing, 'dp', split_axis=0, concat_axis=0, tiled=True)]
    reduce_sum x0 -> x1, other arithmetic: none -> 14.1 us  [body(): jnp.sum(lax.all_gather(mlp_part.astype(jnp.bfloat16), 'tensor'), axis=0)]
  transfers between devices with their start and end apart: 9 -> 9, of which waited for: 9 -> 9; matrix products, arithmetic and copies ran while one was open for 15% -> 10% of each run, Pallas kernels for 0% -> 0%
where the time goes in v1:
time: 762 us; the launch traced here: 761 us
  waiting for transfers between devices  621 us (81%)
  matrix products  47.8 us (6%)
  other arithmetic  43.8 us (6%)
  local copies, waits for them, and re-layouts  25.2 us (3%)
  between operations  14.4 us (2%)
  starting transfers between devices  8.89 us (1%)
    all_gather x1, waiting for transfers between devices, body(): lax.all_gather(mlp_part.astype(jnp.bfloat16), 'tensor')  305 us
    psum x1, waiting for transfers between devices, body(): lax.psum(attn_part.astype(jnp.bfloat16), 'tensor').astype(jnp.float32)  108 us
    all_gather x1, waiting for transfers between devices, body(): full_stream = lax.all_gather(stream, 'tensor', axis=0, tiled=True)  68.2 us
    all_gather x1, waiting for transfers between devices, body(): lax.all_gather(w_gate_up, 'dp', axis=1, tiled=True)  44.9 us
    all_gather x1, waiting for transfers between devices, body(): lax.all_gather(w_qkv, 'dp', axis=1, tiled=True)  37.2 us
    all_gather x1, waiting for transfers between devices, body(): lax.all_gather(w_down, 'dp', axis=1, tiled=True)  32.8 us
    dot_general x2, matrix products, row_folder(): jnp.einsum('td,cdf->ctf', source, piece, preferred_element_type=jnp.float32)  21.9 us
    all_to_all x1, waiting for transfers between devices, write_cache(): lax.all_to_all(outgoing, 'dp', split_axis=0, concat_axis=0, tiled=True)  17.3 us
  transfers between devices with their start and end apart: 9, of which 9 were waited for; matrix products, arithmetic and copies ran while one was open for 10% of the time, Pallas kernels for 0%

profile of v1, /device:TPU:1, one launch (start us, length us, event | category | flops | bytes accessed | tf_op | source)
XLA Modules:
  0.0 761.0 jit_solution(14106033702721702912)
XLA Ops:
  7.9 1.7 copy.27
  9.8 0.7 all-gather.12.cloned.1.call-update
  10.5 0.7 convert_element_type.78
  11.2 0.8 fusion.83
  12.0 1.9 multiply_cosine_fusion
  14.2 2.1 fusion.35
  16.2 68.2 %all-gather.8.cloned.1.call-done = bf16[1024,2048]{1,0:T(8,128)(2,1)} async-done(((bf16[128,2048]{1,0:T(8,128)(2,1)}), bf16[1024,2048]{1,0:T(8,128)(2,1)}) %all-gather.8.cloned.1.call-update) | async-done | bytes 4194320 | tf_op jit(solution)/shard_map/all_gather | solution.py:88
  84.4 3.0 convert_reduce_fusion
  87.9 1.2 fusion.4
  89.1 37.2 %all-gather.10.cloned.1.call-done = bf16[3,2048,256]{1,2,0:T(8,128)(2,1)} async-done(((bf16[3,128,256]{1,2,0:T(8,128)(2,1)}), bf16[3,2048,256]{1,2,0:T(8,128)(2,1)}) %all-gather.10.cloned.1.call-update) | async-done | bytes 3145744 | tf_op jit(solution)/shard_map/all_gather | solution.py:91
  126.3 7.3 fusion.38
  133.9 0.9 slice.112
  134.8 1.0 fusion.81
  135.8 1.4 copy.41
  137.2 2.4 copy.42
  139.5 1.0 fusion.82
  140.6 1.4 copy.39
  141.9 2.4 copy.40
  144.3 1.6 multiply_subtract_fusion
  146.5 0.8 copy-done.7
  147.8 1.3 copy-done.6
  149.2 1.1 fusion.85
  150.2 3.4 fusion.48
  153.7 3.9 fusion.84
  157.6 2.5 fusion.49
  160.1 1.8 all-gather.12.cloned.1.call-done
  161.9 4.5 convolution_convert_fusion
  167.8 108.4 %all-reduce.2.cloned.1.call-done = bf16[1024,2048]{1,0:T(8,128)(2,1)} async-done(((bf16[1024,2048]{1,0:T(8,128)(2,1)}), bf16[1024,2048]{1,0:T(8,128)(2,1)}) %all-reduce.2.cloned.1.call-update) | async-done | bytes 4194320 | tf_op jit(solution)/shard_map/psum | solution.py:99
  276.2 4.8 convert_reduce_fusion.1
  281.0 1.9 copy-done.1
  282.9 1.2 multiply_reduce_fusion
  284.2 44.9 %all-gather.14.cloned.1.call-done = bf16[2,2048,1024]{2,1,0:T(8,128)(2,1)} async-done(((bf16[2,128,1024]{2,1,0:T(8,128)(2,1)}), bf16[2,2048,1024]{2,1,0:T(8,128)(2,1)}) %all-gather.14.cloned.1.call-update) | async-done | bytes 8388624 | tf_op jit(solution)/shard_map/all_gather | solution.py:102
  329.1 14.6 %fusion.23 = f32[2,1024,1024]{2,1,0:T(8,128)} fusion(bf16[2,2048,1024]{2,1,0:T(8,128)(2,1)} %all-gather.14.cloned.1.call-done, bf16[1024,2048]{1,0:T(8,128)(2,1)} %copy-done.1, f32[1024]{0:T(1024)S(1)} %add_rsqrt_fusion, f32[1024]{0:T(1024)S(1)} %broadcast_multiply_fusion), kind=kOutput, calls=%fused_computation.34 | convolution fusion | flops 8598323200 | bytes 20979712 | tf_op jit(solution)/shard_map/td,cdf->ctf/dot_general | solution.py:31
  343.6 32.8 %all-gather.16.cloned.1.call-done = bf16[1024,2048]{1,0:T(8,128)(2,1)} async-done(((bf16[1024,128]{1,0:T(8,128)(2,1)}), bf16[1024,2048]{1,0:T(8,128)(2,1)}) %all-gather.16.cloned.1.call-update) | async-done | bytes 4194320 | tf_op jit(solution)/shard_map/all_gather | solution.py:105
  376.4 11.2 %convolution_convert_fusion.1 = bf16[1024,2048]{1,0:T(8,128)(2,1)} fusion(bf16[1024,2048]{1,0:T(8,128)(2,1)} %all-gather.16.cloned.1.call-done, f32[2,1024,1024]{2,1,0:T(8,128)} %fusion.23), kind=kOutput, calls=%fused_computation.32 | convolution fusion | flops 4303355904 | bytes 16777216 | tf_op jit(solution)/shard_map/dot_general | solution.py:104
  388.2 2.0 sort.17
  390.3 0.8 gather_fusion
  391.0 0.7 all_to_all.9
  391.7 4.3 all-to-all-start
  397.2 1.6 gather_fusion.1
  398.8 2.7 all-to-all-done
  401.5 4.1 all-to-all-start.1
  405.7 17.3 %all-to-all-done.1 = bf16[16,4,2,16,256]{4,3,2,1,0:T(8,128)(2,1)S(1)} async-done(((bf16[16,4,2,16,256]{4,3,2,1,0:T(8,128)(2,1)}), bf16[16,4,2,16,256]{4,3,2,1,0:T(8,128)(2,1)S(1)}, u32[]{:S(2)}, u32[]{:S(2)}) %all-to-all-start.1) | async-done | bytes 1048608 | tf_op jit(solution)/shard_map/all_to_all | solution.py:77
  423.1 2.5 scatter_fusion
  425.6 6.8 convert_element_type.88
  432.5 305.4 %all-gather.18.cloned.1.call-done = bf16[8192,2048]{1,0:T(8,128)(2,1)} async-done(((bf16[1024,2048]{1,0:T(8,128)(2,1)}), bf16[8192,2048]{1,0:T(8,128)(2,1)}) %all-gather.18.cloned.1.call-update) | async-done | bytes 33554448 | tf_op jit(solution)/shard_map/all_gather | solution.py:107
  737.8 14.1 %reduce_sum.72 = bf16[1024,2048]{1,0:T(8,128)(2,1)} reduce(bf16[8,1024,2048]{2,1,0:T(8,128)(2,1)} %bitcast.67, bf16[]{:T(256)} %constant.51.clone.1), dimensions={0}, to_apply=%region_9.10 | reduce | flops 14680064 | bytes 37748736 | tf_op jit(solution)/shard_map/reduce_sum | solution.py:107
  751.9 2.3 fusion.52
  (59 shorter events, 6.6 us)
Async XLA Ops:
  7.2 77.3 %all-gather.8.cloned.1.call-start = ((), (), s32[]{:S(2)}) async-start(), calls=%async_computation.2 | async-start | bytes 4718592 | tf_op jit(solution)/shard_map/all_gather | solution.py:88
  7.9 118.4 %all-gather.10.cloned.1.call-start = ((), (), s32[]{:S(2)}) async-start(), calls=%async_computation.3 | async-start | bytes 3342336 | tf_op jit(solution)/shard_map/all_gather | solution.py:91
  9.7 152.2 %all-gather.12.cloned.1.call-start = ((), (), s32[]{:S(2)}) async-start(), calls=%async_computation.4 | async-start | bytes 1114112 | tf_op jit(solution)/shard_map/all_gather | solution.py:97
  10.4 265.8 %all-reduce.2.cloned.1.call-start = ((), (), s32[]{:S(2)}) async-start(), calls=%async_computation.5 | async-start | bytes 8388608 | tf_op jit(solution)/shard_map/psum | solution.py:99
  84.4 3.4 copy-start.2
  144.3 1.9 copy-start.4
  146.5 0.8 copy-start.7
  147.3 3.0 slice-start
  147.8 1.3 copy-start.6
  149.2 4.5 copy-start.8
  149.2 4.5 copy-start.9
  153.6 3.9 copy-start.5
  166.4 162.6 %all-gather.14.cloned.1.call-start = ((), (), s32[]{:S(2)}) async-start(), calls=%async_computation.6 | async-start | bytes 8912896 | tf_op jit(solution)/shard_map/all_gather | solution.py:102
  167.0 209.4 %all-gather.16.cloned.1.call-start = ((), (), s32[]{:S(2)}) async-start(), calls=%async_computation.7 | async-start | bytes 4456448 | tf_op jit(solution)/shard_map/all_gather | solution.py:105
  167.6 570.3 %all-gather.18.cloned.1.call-start = ((), (), s32[]{:S(2)}) async-start(), calls=%async_computation.8 | async-start | bytes 37748736 | tf_op jit(solution)/shard_map/all_gather | solution.py:107
  281.0 1.9 copy-start.1
  387.6 0.7 copy-start
  391.7 9.7 %all-to-all-start = ((s32[16,1,4]{2,1,0:T(1,128)}), s32[16,1,4]{2,1,0:T(1,128)S(1)}, u32[]{:S(2)}, u32[]{:S(2)}) async-start(s32[16,1,4]{2,1,0:T(1,128)} %bitcast.16), calls=%async_computation | async-start | bytes 16384 | tf_op jit(solution)/shard_map/all_to_all | solution.py:78
  401.5 21.5 %all-to-all-start.1 = ((bf16[16,4,2,16,256]{4,3,2,1,0:T(8,128)(2,1)}), bf16[16,4,2,16,256]{4,3,2,1,0:T(8,128)(2,1)S(1)}, u32[]{:S(2)}, u32[]{:S(2)}) async-start(bf16[16,4,2,16,256]{4,3,2,1,0:T(8,128)(2,1)} %bitcast.22), calls=%async_computation.1 | async-start | bytes 2097152 | tf_op jit(solution)/shard_map/all_to_all | solution.py:77
  425.6 6.9 copy-start.3
Sparse Core Ops, SparseCore 0:
  10.3 74.0 all-gather.7
  86.6 39.6 all-gather.9
  127.9 33.9 all-gather.11
  166.5 109.6 all-reduce.1
  277.8 51.2 all-gather.13
  330.5 45.8 all-gather.15
  387.7 350.0 all-gather.17
